TPU v7x, 512 devices: a whole 4x8x8 slice. The times are simulated.
512 devices in a mesh: head: 16 (over y, core), seq: 32 (over z, x).
Axes of the slice: x: 4, y: 8, z: 8, core: 2. Of those that a mesh axis runs over, the one named last changes fastest.
Arguments:
- queries: bfloat16 [32768, 2048], P(('seq', 'head'))
- keys: bfloat16 [32768, 2048], P(('seq', 'head'))
- values: bfloat16 [32768, 2048], P(('seq', 'head')), may hold values from -6 to 6
- grad_out: bfloat16 [32768, 2048], P(('seq', 'head')), may hold values from -6 to 6
- random_blocks: int32 [256, 3], P('seq'), may hold values from 0 to 255, as said below
Outputs:
- attended: bfloat16 [32768, 2048], P(('seq', 'head'))
- grad_queries: bfloat16 [32768, 2048], P(('seq', 'head'))
- grad_keys: bfloat16 [32768, 2048], P(('seq', 'head'))
- grad_values: bfloat16 [32768, 2048], P(('seq', 'head'))
Inputs may be any that keep to these rules, and one draw needn't show every extreme that they name: `random_blocks`: within the rows of one sequence group (8 consecutive query blocks), at most 2 entries name blocks of any one group's range of 8 blocks, and in every group's rows one group's range is named exactly 2 times.
All inputs are finite; a program needn't handle non-finite values.
Results may differ from a plain program's by a relative error of at most 0.022.
Values may be sent and summed in bfloat16 or wider, within the bound.
No kernel may reach another device: no remote copies, remote signals or barrier semaphores. Data moves between devices by JAX's collectives and lax.ppermute only.
A program may use at most 192 MiB of HBM per device.

v0:
```python
import jax
import jax.numpy as jnp
from jax import lax
from jax.sharding import PartitionSpec as P

HD = 128
BLK = 128
RAND = 3


def with_halo(cells, sides, width):
    for axis, dim in sides:
        count = lax.axis_size(axis)
        ends = count - 1
        head = lax.slice_in_dim(cells, 0, width, axis=dim)
        tail = lax.slice_in_dim(cells, cells.shape[dim] - width, cells.shape[dim], axis=dim)
        cells = jnp.concatenate(
            [
                lax.ppermute(tail, axis, [(i, (i + 1) % count) for i in range(ends)]),
                cells,
                lax.ppermute(head, axis, [((i + 1) % count, i) for i in range(ends)]),
            ],
            axis=dim,
        )
    return cells


def broadcast(value, axis):
    count = lax.axis_size(axis)
    me = lax.axis_index(axis)
    step = 1
    while step < count:
        pairs = [(i, i + step) for i in range(step) if i + step < count]
        got = lax.ppermute(value, axis, pairs)
        value = jnp.where((me >= step) & (me < 2 * step), got, value)
        step *= 2
    return value


def reduce_to_first(value, axis):
    count = lax.axis_size(axis)
    step = 1
    while step * 2 < count:
        step *= 2
    while step >= 1:
        pairs = [(i + step, i) for i in range(step) if i + step < count]
        value = value + lax.ppermute(value, axis, pairs)
        step //= 2
    return value


def slot_places(owners, groups, capacity):
    owner_hits = (owners[:, None] == jnp.arange(groups, dtype=jnp.int32)[None, :]).astype(jnp.int32)
    earlier = jnp.cumsum(owner_hits, axis=0) - owner_hits
    return owners * capacity + jnp.sum(earlier * owner_hits, axis=1)


def request_table(list_rows, query_count, groups, capacity):
    flat_rows = list_rows.reshape(-1)
    places = slot_places(flat_rows // query_count, groups, capacity)
    matches = places[None, :] == jnp.arange(groups * capacity, dtype=jnp.int32)[:, None]
    table = jnp.sum(jnp.where(matches, (flat_rows % query_count)[None, :], 0), axis=1)
    return table.reshape(groups, capacity)


def window_valid(my_group, query_count, groups):
    block_ids = jnp.arange(query_count, dtype=jnp.int32)
    left_ok = jnp.logical_not(jnp.logical_and(my_group == 0, block_ids == 0))
    right_ok = jnp.logical_not(
        jnp.logical_and(my_group == groups - 1, block_ids == query_count - 1)
    )
    all_true = jnp.ones((query_count, BLK), dtype=bool)
    return jnp.concatenate(
        [
            all_true,
            all_true,
            left_ok[:, None] & all_true,
            all_true,
            right_ok[:, None] & all_true,
            jnp.ones((query_count, RAND * BLK), dtype=bool),
        ],
        axis=1,
    )


def against_keys(rows, global_part, window_part, remote_part):
    return jnp.concatenate(
        [
            jnp.einsum("qihd,jhd->qhij", rows, global_part, preferred_element_type=jnp.float32),
            jnp.einsum("qihd,qjhd->qhij", rows, window_part, preferred_element_type=jnp.float32),
            jnp.einsum("qihd,qjhd->qhij", rows, remote_part, preferred_element_type=jnp.float32),
        ],
        axis=-1,
    )


def split_keys(table):
    return (table[..., : 2 * BLK], table[..., 2 * BLK : 5 * BLK], table[..., 5 * BLK :])


def weigh_keys(table, global_part, window_part, remote_part):
    global_w, window_w, random_w = split_keys(table)
    return (
        jnp.einsum("qhij,jhd->qihd", global_w, global_part, preferred_element_type=jnp.float32)
        + jnp.einsum("qhij,qjhd->qihd", window_w, window_part, preferred_element_type=jnp.float32)
        + jnp.einsum("qhij,qjhd->qihd", random_w, remote_part, preferred_element_type=jnp.float32)
    )


def key_terms(table, rows):
    global_w, window_w, random_w = split_keys(table)
    return (
        jnp.einsum("qhij,qihd->jhd", global_w, rows, preferred_element_type=jnp.float32),
        jnp.einsum("qhij,qihd->qjhd", window_w, rows, preferred_element_type=jnp.float32),
        jnp.einsum("qhij,qihd->qjhd", random_w, rows, preferred_element_type=jnp.float32),
    )


def shards(queries, keys, values, grad_out, random_blocks):
    groups = lax.axis_size("seq")
    my_group = lax.axis_index("seq")
    head_q, head_k, head_v, head_g = (
        lax.all_to_all(queries, "head", split_axis=1, concat_axis=0, tiled=True),
        lax.all_to_all(keys, "head", split_axis=1, concat_axis=0, tiled=True),
        lax.all_to_all(values, "head", split_axis=1, concat_axis=0, tiled=True),
        lax.all_to_all(grad_out, "head", split_axis=1, concat_axis=0, tiled=True),
    )
    group_tokens = head_q.shape[0]
    head_count = head_q.shape[1] // HD
    query_count = group_tokens // BLK
    capacity = max(2, 3 * query_count * RAND // (2 * groups))
    score_scale = HD ** (-0.5)
    key_value = jnp.stack([head_k, head_v])
    kv_blocks = key_value.reshape(2, query_count, BLK, head_count, HD)
    edged = with_halo(key_value, (("seq", 1),), BLK)
    edged = edged.reshape(2, query_count + 2, BLK, head_count, HD)
    window_kv = jnp.concatenate(
        [edged[:, 0:query_count], edged[:, 1 : query_count + 1], edged[:, 2 : query_count + 2]],
        axis=2,
    )
    global_kv = broadcast(kv_blocks[:, 0:2].reshape(2, 2 * BLK, head_count, HD), "seq")
    flat_ids = random_blocks.reshape(-1)
    places = slot_places(flat_ids // query_count, groups, capacity)
    wanted = lax.all_to_all(
        request_table(random_blocks, query_count, groups, capacity),
        "seq",
        split_axis=0,
        concat_axis=0,
        tiled=True,
    )
    served = jnp.take(kv_blocks, wanted.reshape(-1), axis=1)
    served = served.reshape(2, groups, capacity, BLK, head_count, HD)
    fetched = lax.all_to_all(served, "seq", split_axis=1, concat_axis=1, tiled=True)
    chosen = jnp.take(fetched.reshape(2, groups * capacity, BLK, head_count, HD), places, axis=1)
    remote_kv = chosen.reshape(2, query_count, RAND * BLK, head_count, HD)
    query_blocks = head_q.reshape(query_count, BLK, head_count, HD)
    grad_blocks = head_g.reshape(query_count, BLK, head_count, HD)
    scores = score_scale * against_keys(query_blocks, global_kv[0], window_kv[0], remote_kv[0])
    valid = window_valid(my_group, query_count, groups)
    scores = jnp.where(valid[:, None, None, :], scores, -jnp.inf)
    row_max = jnp.max(scores, axis=-1, keepdims=True)
    exponent = jnp.exp(scores - row_max)
    attention_probs = exponent / jnp.sum(exponent, axis=-1, keepdims=True)
    weights = attention_probs.astype(jnp.bfloat16)
    attended = weigh_keys(weights, global_kv[1], window_kv[1], remote_kv[1]).astype(jnp.bfloat16)
    grad_prob = against_keys(grad_blocks, global_kv[1], window_kv[1], remote_kv[1])
    row_delta = jnp.sum(attention_probs * grad_prob, axis=-1, keepdims=True)
    grad_score = (score_scale * attention_probs * (grad_prob - row_delta)).astype(jnp.bfloat16)
    grad_q = weigh_keys(grad_score, global_kv[0], window_kv[0], remote_kv[0]).astype(jnp.bfloat16)
    key_global, key_window, key_random = key_terms(grad_score, query_blocks)
    value_global, value_window, value_random = key_terms(weights, grad_blocks)
    global_sum = reduce_to_first(jnp.stack([key_global, value_global]), "seq")
    window_grad = jnp.stack([key_window, value_window]).reshape(
        2, query_count, 3, BLK, head_count, HD
    )
    no_pad = (0, 0)
    extended = (
        jnp.pad(window_grad[:, :, 0], (no_pad, (0, 2), no_pad, no_pad, no_pad))
        + jnp.pad(window_grad[:, :, 1], (no_pad, (1, 1), no_pad, no_pad, no_pad))
        + jnp.pad(window_grad[:, :, 2], (no_pad, (2, 0), no_pad, no_pad, no_pad))
    )
    outward = jnp.concatenate([extended[:, 0], extended[:, query_count + 1]], axis=1)
    inward = with_halo(outward.astype(jnp.bfloat16), (("seq", 1),), BLK).astype(outward.dtype)
    own_grad = extended[:, 1 : query_count + 1]
    own_grad = own_grad.at[:, 0].add(inward[:, :BLK])
    own_grad = own_grad.at[:, query_count - 1].add(inward[:, 3 * BLK :])
    random_terms = (
        jnp.stack([key_random, value_random])
        .reshape(2, query_count * RAND, BLK, head_count, HD)
        .astype(jnp.bfloat16)
    )
    send_pick = (places[None, :] == jnp.arange(groups * capacity, dtype=jnp.int32)[:, None]).astype(
        jnp.bfloat16
    )
    outgoing = jnp.einsum(
        "pj,xjihd->xpihd", send_pick, random_terms, preferred_element_type=jnp.float32
    ).astype(jnp.bfloat16)
    incoming = lax.all_to_all(
        outgoing.reshape(2, groups, capacity, BLK, head_count, HD),
        "seq",
        split_axis=1,
        concat_axis=1,
        tiled=True,
    )
    take_pick = (
        wanted.reshape(-1)[None, :] == jnp.arange(query_count, dtype=jnp.int32)[:, None]
    ).astype(jnp.bfloat16)
    random_sum = jnp.einsum(
        "qp,xpihd->xqihd",
        take_pick,
        incoming.reshape(2, groups * capacity, BLK, head_count, HD),
        preferred_element_type=jnp.float32,
    )
    global_sum = global_sum.reshape(2, 2, BLK, head_count, HD)
    own_grad = own_grad.at[:, 0:2].add(jnp.where(my_group == 0, global_sum, 0.0))
    total_grad = own_grad + random_sum
    grad_k = total_grad[0].reshape(group_tokens, head_count * HD).astype(jnp.bfloat16)
    grad_v = total_grad[1].reshape(group_tokens, head_count * HD).astype(jnp.bfloat16)
    return (
        lax.all_to_all(
            attended.reshape(group_tokens, head_count * HD),
            "head",
            split_axis=0,
            concat_axis=1,
            tiled=True,
        ),
        lax.all_to_all(
            grad_q.reshape(group_tokens, head_count * HD),
            "head",
            split_axis=0,
            concat_axis=1,
            tiled=True,
        ),
        lax.all_to_all(grad_k, "head", split_axis=0, concat_axis=1, tiled=True),
        lax.all_to_all(grad_v, "head", split_axis=0, concat_axis=1, tiled=True),
    )


def solution(mesh):
    placed = (
        P(("seq", "head"), None),
        P(("seq", "head"), None),
        P(("seq", "head"), None),
        P(("seq", "head"), None),
        P("seq", None),
    )
    return jax.shard_map(
        shards,
        mesh=mesh,
        in_specs=placed,
        out_specs=(
            P(("seq", "head"), None),
            P(("seq", "head"), None),
            P(("seq", "head"), None),
            P(("seq", "head"), None),
        ),
        check_vma=False,
    )
```

profile of v0, /device:TPU:3, one launch (start us, length us, event | category | flops | bytes accessed | tf_op | source)
XLA Modules:
  0.0 459.8 jit_solution(10940676813869439960)
XLA Ops:
  2.7 12.9 %all-to-all-start.3 = ((s32[32,1,2]{2,1,0:T(1,128)}), s32[32,1,2]{2,1,0:T(1,128)S(1)}, u32[]{:S(2)}, u32[]{:S(2)}) async-start(s32[32,1,2]{2,1,0:T(1,128)} %bitcast.20), calls=%async_computation.3 | async-start | bytes 32768 | tf_op jit(solution)/shard_map/all_to_all | solution.py:144
  16.4 6.8 %all-to-all-done.3 = s32[32,1,2]{2,1,0:T(1,128)S(1)} async-done(((s32[32,1,2]{2,1,0:T(1,128)}), s32[32,1,2]{2,1,0:T(1,128)S(1)}, u32[]{:S(2)}, u32[]{:S(2)}) %all-to-all-start.3) | async-done | bytes 288 | tf_op jit(solution)/shard_map/all_to_all | solution.py:144
  23.2 9.2 %all-to-all-start.2 = ((bf16[64,16,128]{2,0,1:T(8,128)(2,1)}), bf16[64,16,128]{2,0,1:T(8,128)(2,1)S(1)}, u32[]{:S(2)}, u32[]{:S(2)}) async-start(bf16[64,16,128]{2,0,1:T(8,128)(2,1)} %copy_bitcast_fusion.8), calls=%async_computation.2 | async-start | bytes 524288 | tf_op jit(solution)/shard_map/all_to_all | solution.py:123
  32.4 1.7 copy_bitcast_fusion.10
  34.2 10.0 %all-to-all-done.2 = bf16[64,16,128]{2,0,1:T(8,128)(2,1)S(1)} async-done(((bf16[64,16,128]{2,0,1:T(8,128)(2,1)}), bf16[64,16,128]{2,0,1:T(8,128)(2,1)S(1)}, u32[]{:S(2)}, u32[]{:S(2)}) %all-to-all-start.2) | async-done | bytes 262176 | tf_op jit(solution)/shard_map/all_to_all | solution.py:123
  44.1 3.4 all-to-all-start
  50.5 8.2 %all-to-all-done = bf16[64,16,128]{2,0,1:T(8,128)(2,1)S(1)} async-done(((bf16[64,16,128]{2,0,1:T(8,128)(2,1)}), bf16[64,16,128]{2,0,1:T(8,128)(2,1)S(1)}, u32[]{:S(2)}, u32[]{:S(2)}) %all-to-all-start) | async-done | bytes 262176 | tf_op jit(solution)/shard_map/all_to_all | solution.py:124
  58.7 3.4 all-to-all-start.1
  62.3 11.6 %all-to-all-done.1 = bf16[64,16,128]{2,0,1:T(8,128)(2,1)S(1)} async-done(((bf16[64,16,128]{2,0,1:T(8,128)(2,1)}), bf16[64,16,128]{2,0,1:T(8,128)(2,1)S(1)}, u32[]{:S(2)}, u32[]{:S(2)}) %all-to-all-start.1) | async-done | bytes 262176 | tf_op jit(solution)/shard_map/all_to_all | solution.py:125
  73.8 3.4 all-to-all-start.6
  77.3 3.1 gather_fusion
  80.4 2.7 copy.169
  83.6 2.5 copy.170
  86.1 2.3 all-to-all-done.6
  88.4 5.6 %all-to-all-start.4 = ((bf16[2,32,2,128,1,128]{5,3,2,0,4,1:T(8,128)(2,1)}), bf16[2,32,2,128,1,128]{5,3,2,0,4,1:T(8,128)(2,1)}, u32[]{:S(2)}, u32[]{:S(2)}) async-start(bf16[2,32,2,128,1,128]{5,3,2,0,4,1:T(8,128)(2,1)} %copy.170), calls=%async_computation.4 | async-start | bytes 8388608 | tf_op jit(solution)/shard_map/all_to_all | solution.py:153
  94.4 3.1 collective-permute-start.5
  97.5 2.2 collective-permute-start.6
  101.0 7.7 %collective-permute-done.5 = bf16[2,128,128]{2,1,0:T(8,128)(2,1)S(1)} collective-permute-done((bf16[2,128,128]{2,1,0:T(8,128)(2,1)S(1)}, bf16[2,128,128]{2,1,0:T(8,128)(2,1)S(1)}, u32[]{:S(2)}, u32[]{:S(2)}) %collective-permute-start.5) | collective-permute-done | bytes 65568 | tf_op jit(solution)/shard_map/ppermute | solution.py:19
  108.7 3.4 collective-permute-done
  112.1 78.6 %collective-permute-start.1 = (bf16[2,256,1,128]{3,1,2,0:T(8,128)(2,1)S(1)}, bf16[2,256,1,128]{3,1,2,0:T(8,128)(2,1)S(1)}, u32[]{:S(2)}, u32[]{:S(2)}) collective-permute-start(bf16[2,256,1,128]{3,1,2,0:T(8,128)(2,1)S(1)} %broadcast_select_fusion.1), channel_id=1, source_target_pairs={{0,2},{1,3},{32,34},{33,35},{64,66},{65,67},{96,98},{97,99},{128,1... | collective-permute-start | bytes 393224 | tf_op jit(solution)/shard_map/ppermute | solution.py:34
  191.1 1.6 collective-permute-done.1
  194.1 1.8 collective-permute-done.2
  197.6 1.6 collective-permute-done.3
  204.7 4.8 %copy.171 = bf16[2,32,2,128,1,128]{5,3,2,1,0,4:T(8,128)(2,1)} copy(bf16[2,32,2,128,1,128]{5,3,2,0,4,1:T(8,128)(2,1)} %all-to-all-done.4) | data formatting | bytes 8388608 | tf_op jit(solution)/shard_map/all_to_all | solution.py:153
  209.5 4.1 gather_fusion.1
  213.6 1.6 bitcast_select_fusion
  220.4 1.9 multiply_reduce_fusion
  222.3 2.3 multiply_convert_fusion
  228.6 6.7 %copy.190 = bf16[2,32,2,128,1,128]{5,2,3,0,4,1:T(2,128)(2,1)} copy(bf16[2,32,2,128,1,128]{5,2,1,3,0,4:T(2,128)(2,1)S(1)} %bitcast.311) | data formatting | bytes 8388608 | tf_op jit(solution)/shard_map/reshape | solution.py:199
  235.3 17.6 %all-to-all-start.8 = ((bf16[2,32,2,128,1,128]{5,2,3,0,4,1:T(2,128)(2,1)}), bf16[2,32,2,128,1,128]{5,2,3,0,4,1:T(2,128)(2,1)}, u32[]{:S(2)}, u32[]{:S(2)}) async-start(bf16[2,32,2,128,1,128]{5,2,3,0,4,1:T(2,128)(2,1)} %copy.190), calls=%async_computation.8 | async-start | bytes 8388608 | tf_op jit(solution)/shard_map/all_to_all | solution.py:198
  259.9 93.3 %collective-permute-done.9 = f32[2,256,1,128]{3,1,2,0:T(8,128)S(1)} collective-permute-done((f32[2,256,1,128]{3,1,2,0:T(8,128)S(1)}, f32[2,256,1,128]{3,1,2,0:T(8,128)S(1)}, u32[]{:S(2)}, u32[]{:S(2)}) %collective-permute-start.9) | collective-permute-done | bytes 262176 | tf_op jit(solution)/shard_map/ppermute | solution.py:47
  355.1 3.5 collective-permute-start.7
  358.6 1.9 collective-permute-start.8
  361.0 5.7 %collective-permute-done.10 = f32[2,256,1,128]{3,1,2,0:T(8,128)S(1)} collective-permute-done((f32[2,256,1,128]{3,1,2,0:T(8,128)S(1)}, f32[2,256,1,128]{3,1,2,0:T(8,128)S(1)}, u32[]{:S(2)}, u32[]{:S(2)}) %collective-permute-start.10) | collective-permute-done | bytes 262176 | tf_op jit(solution)/shard_map/ppermute | solution.py:47
  369.1 5.5 %collective-permute-done.11 = f32[2,256,1,128]{3,1,2,0:T(8,128)S(1)} collective-permute-done((f32[2,256,1,128]{3,1,2,0:T(8,128)S(1)}, f32[2,256,1,128]{3,1,2,0:T(8,128)S(1)}, u32[]{:S(2)}, u32[]{:S(2)}) %collective-permute-start.11) | collective-permute-done | bytes 262176 | tf_op jit(solution)/shard_map/ppermute | solution.py:47
  377.0 6.3 %collective-permute-done.12 = f32[2,256,1,128]{3,1,2,0:T(8,128)S(1)} collective-permute-done((f32[2,256,1,128]{3,1,2,0:T(8,128)S(1)}, f32[2,256,1,128]{3,1,2,0:T(8,128)S(1)}, u32[]{:S(2)}, u32[]{:S(2)}) %collective-permute-start.12) | collective-permute-done | bytes 262176 | tf_op jit(solution)/shard_map/ppermute | solution.py:47
  383.3 3.4 collective-permute-start.13
  387.5 3.0 scatter-add.11
  390.5 10.5 %all-to-all-start.5 = ((bf16[16,64,128]{2,1,0:T(8,128)(2,1)}), bf16[16,64,128]{2,1,0:T(8,128)(2,1)S(1)}, u32[]{:S(2)}, u32[]{:S(2)}) async-start(bf16[16,64,128]{2,1,0:T(8,128)(2,1)} %bitcast.45), calls=%async_computation.5 | async-start | bytes 524288 | tf_op jit(solution)/shard_map/all_to_all | solution.py:220
  401.4 9.0 %copy.191 = bf16[2,32,2,128,1,128]{5,2,1,3,0,4:T(2,128)(2,1)} copy(bf16[2,32,2,128,1,128]{5,2,3,0,4,1:T(2,128)(2,1)} %all-to-all-done.8) | data formatting | bytes 8388608 | tf_op jit(solution)/shard_map/all_to_all | solution.py:198
  410.4 2.5 all-to-all-done.5
  412.9 4.8 %all-to-all-start.7 = ((bf16[16,64,128]{2,1,0:T(8,128)(2,1)}), bf16[16,64,128]{2,1,0:T(8,128)(2,1)S(1)}, u32[]{:S(2)}, u32[]{:S(2)}) async-start(bf16[16,64,128]{2,1,0:T(8,128)(2,1)} %bitcast.67), calls=%async_computation.7 | async-start | bytes 524288 | tf_op jit(solution)/shard_map/all_to_all | solution.py:227
  417.7 2.8 fusion.7
  421.3 8.1 %all-to-all-done.7 = bf16[16,64,128]{2,1,0:T(8,128)(2,1)S(1)} async-done(((bf16[16,64,128]{2,1,0:T(8,128)(2,1)}), bf16[16,64,128]{2,1,0:T(8,128)(2,1)S(1)}, u32[]{:S(2)}, u32[]{:S(2)}) %all-to-all-start.7) | async-done | bytes 262176 | tf_op jit(solution)/shard_map/all_to_all | solution.py:227
  429.4 3.4 all-to-all-start.10
  434.3 9.6 %all-to-all-done.10 = bf16[16,64,128]{2,1,0:T(8,128)(2,1)S(1)} async-done(((bf16[16,64,128]{2,1,0:T(8,128)(2,1)}), bf16[16,64,128]{2,1,0:T(8,128)(2,1)S(1)}, u32[]{:S(2)}, u32[]{:S(2)}) %all-to-all-start.10) | async-done | bytes 262176 | tf_op jit(solution)/shard_map/all_to_all | solution.py:235
  443.9 3.4 all-to-all-start.9
  448.8 10.2 %all-to-all-done.9 = bf16[16,64,128]{2,1,0:T(8,128)(2,1)S(1)} async-done(((bf16[16,64,128]{2,1,0:T(8,128)(2,1)}), bf16[16,64,128]{2,1,0:T(8,128)(2,1)S(1)}, u32[]{:S(2)}, u32[]{:S(2)}) %all-to-all-start.9) | async-done | bytes 262176 | tf_op jit(solution)/shard_map/all_to_all | solution.py:234
  (145 shorter events, 45.6 us)
Async XLA Ops:
  0.6 15.0 %copy-start = (bf16[64,2048]{1,0:T(8,128)(2,1)S(1)}, bf16[64,2048]{1,0:T(8,128)(2,1)}, u32[]{:S(2)}) copy-start(bf16[64,2048]{1,0:T(8,128)(2,1)} %param.11) | copy-start | bytes 786436
  0.6 46.9 %copy-start.16 = (bf16[64,2048]{1,0:T(8,128)(2,1)S(1)}, bf16[64,2048]{1,0:T(8,128)(2,1)}, u32[]{:S(2)}) copy-start(bf16[64,2048]{1,0:T(8,128)(2,1)} %param.13) | copy-start | bytes 786436
  0.7 47.7 %copy-start.17 = (bf16[64,2048]{1,0:T(8,128)(2,1)S(1)}, bf16[64,2048]{1,0:T(8,128)(2,1)}, u32[]{:S(2)}) copy-start(bf16[64,2048]{1,0:T(8,128)(2,1)} %param.14) | copy-start | bytes 786436
  2.7 20.5 %all-to-all-start.3 = ((s32[32,1,2]{2,1,0:T(1,128)}), s32[32,1,2]{2,1,0:T(1,128)S(1)}, u32[]{:S(2)}, u32[]{:S(2)}) async-start(s32[32,1,2]{2,1,0:T(1,128)} %bitcast.20), calls=%async_computation.3 | async-start | bytes 32768 | tf_op jit(solution)/shard_map/all_to_all | solution.py:144
  23.2 20.9 %all-to-all-start.2 = ((bf16[64,16,128]{2,0,1:T(8,128)(2,1)}), bf16[64,16,128]{2,0,1:T(8,128)(2,1)S(1)}, u32[]{:S(2)}, u32[]{:S(2)}) async-start(bf16[64,16,128]{2,0,1:T(8,128)(2,1)} %copy_bitcast_fusion.8), calls=%async_computation.2 | async-start | bytes 524288 | tf_op jit(solution)/shard_map/all_to_all | solution.py:123
  44.1 14.6 %all-to-all-start = ((bf16[64,16,128]{2,0,1:T(8,128)(2,1)}), bf16[64,16,128]{2,0,1:T(8,128)(2,1)S(1)}, u32[]{:S(2)}, u32[]{:S(2)}) async-start(bf16[64,16,128]{2,0,1:T(8,128)(2,1)} %copy_bitcast_fusion.10), calls=%async_computation | async-start | bytes 524288 | tf_op jit(solution)/shard_map/all_to_all | solution.py:124
  58.7 15.1 %all-to-all-start.1 = ((bf16[64,16,128]{2,0,1:T(8,128)(2,1)}), bf16[64,16,128]{2,0,1:T(8,128)(2,1)S(1)}, u32[]{:S(2)}, u32[]{:S(2)}) async-start(bf16[64,16,128]{2,0,1:T(8,128)(2,1)} %copy_bitcast_fusion.9), calls=%async_computation.1 | async-start | bytes 524288 | tf_op jit(solution)/shard_map/all_to_all | solution.py:125
  73.8 14.5 %all-to-all-start.6 = ((bf16[64,16,128]{2,0,1:T(8,128)(2,1)}), bf16[64,16,128]{2,0,1:T(8,128)(2,1)S(1)}, u32[]{:S(2)}, u32[]{:S(2)}) async-start(bf16[64,16,128]{2,0,1:T(8,128)(2,1)} %copy_bitcast_fusion.7), calls=%async_computation.6 | async-start | bytes 524288 | tf_op jit(solution)/shard_map/all_to_all | solution.py:126
  88.4 116.3 %all-to-all-start.4 = ((bf16[2,32,2,128,1,128]{5,3,2,0,4,1:T(8,128)(2,1)}), bf16[2,32,2,128,1,128]{5,3,2,0,4,1:T(8,128)(2,1)}, u32[]{:S(2)}, u32[]{:S(2)}) async-start(bf16[2,32,2,128,1,128]{5,3,2,0,4,1:T(8,128)(2,1)} %copy.170), calls=%async_computation.4 | async-start | bytes 8388608 | tf_op jit(solution)/shard_map/all_to_all | solution.py:153
  94.4 14.3 %collective-permute-start.5 = (bf16[2,128,128]{2,1,0:T(8,128)(2,1)S(1)}, bf16[2,128,128]{2,1,0:T(8,128)(2,1)S(1)}, u32[]{:S(2)}, u32[]{:S(2)}) collective-permute-start(bf16[2,128,128]{2,1,0:T(8,128)(2,1)S(1)} %get-tuple-element.58), channel_id=1, source_target_pairs={{0,1},{1,2},{2,3},{3,4},{4,5},{5,6},{6,7},{7,8},{8,9},{9,10},{10,1... | collective-permute-start | bytes 196616 | tf_op jit(solution)/shard_map/ppermute | solution.py:19
  97.5 11.2 %collective-permute-start.6 = (bf16[2,128,128]{2,1,0:T(8,128)(2,1)S(1)}, bf16[2,128,128]{2,1,0:T(8,128)(2,1)S(1)}, u32[]{:S(2)}, u32[]{:S(2)}) collective-permute-start(bf16[2,128,128]{2,1,0:T(8,128)(2,1)S(1)} %get-tuple-element.59), channel_id=1, source_target_pairs={{1,0},{2,1},{3,2},{4,3},{5,4},{6,5},{7,6},{8,7},{9,8},{10,9},{11,1... | collective-permute-start | bytes 196616 | tf_op jit(solution)/shard_map/ppermute | solution.py:21
  99.7 12.4 %collective-permute-start = (bf16[2,256,1,128]{3,1,2,0:T(8,128)(2,1)S(1)}, bf16[2,256,1,128]{3,1,2,0:T(8,128)(2,1)S(1)}, u32[]{:S(2)}, u32[]{:S(2)}) collective-permute-start(bf16[2,256,1,128]{3,1,2,0:T(8,128)(2,1)S(1)} %bitcast.347), channel_id=1, source_target_pairs={{0,1},{32,33},{64,65},{96,97},{128,129},{160,161},{192,193},{224,2... | collective-permute-start | bytes 393224 | tf_op jit(solution)/shard_map/ppermute | solution.py:34
  112.1 80.5 %collective-permute-start.1 = (bf16[2,256,1,128]{3,1,2,0:T(8,128)(2,1)S(1)}, bf16[2,256,1,128]{3,1,2,0:T(8,128)(2,1)S(1)}, u32[]{:S(2)}, u32[]{:S(2)}) collective-permute-start(bf16[2,256,1,128]{3,1,2,0:T(8,128)(2,1)S(1)} %broadcast_select_fusion.1), channel_id=1, source_target_pairs={{0,2},{1,3},{32,34},{33,35},{64,66},{65,67},{96,98},{97,99},{128,1... | collective-permute-start | bytes 393224 | tf_op jit(solution)/shard_map/ppermute | solution.py:34
  192.6 3.2 collective-permute-start.2
  194.1 8.1 %copy-start.6 = (bf16[2,8,384,1,128]{4,2,1,3,0:T(8,128)(2,1)}, bf16[2,8,384,1,128]{4,2,1,3,0:T(8,128)(2,1)S(1)}, u32[]{:S(2)}) copy-start(bf16[2,8,384,1,128]{4,2,1,3,0:T(8,128)(2,1)S(1)} %pad_maximum_fusion.1) | copy-start | bytes 4718596
  195.9 3.3 collective-permute-start.3
  199.2 3.8 collective-permute-start.4
  215.4 1.8 copy-start.10
  215.4 3.3 copy-start.12
  218.7 1.4 copy-start.8
  218.7 1.7 copy-start.9
  224.7 1.4 copy-start.2
  224.7 2.0 copy-start.4
  235.3 17.7 %copy-start.3 = (bf16[8,1,128,1024]{2,3,0,1:T(8,128)(2,1)S(1)}, bf16[8,1,128,1024]{2,3,0,1:T(8,128)(2,1)}, u32[]{:S(2)}) copy-start(bf16[8,1,128,1024]{2,3,0,1:T(8,128)(2,1)} %copy-done.2) | copy-start | bytes 6291460
  235.3 155.3 %all-to-all-start.8 = ((bf16[2,32,2,128,1,128]{5,2,3,0,4,1:T(2,128)(2,1)}), bf16[2,32,2,128,1,128]{5,2,3,0,4,1:T(2,128)(2,1)}, u32[]{:S(2)}, u32[]{:S(2)}) async-start(bf16[2,32,2,128,1,128]{5,2,3,0,4,1:T(2,128)(2,1)} %copy.190), calls=%async_computation.8 | async-start | bytes 8388608 | tf_op jit(solution)/shard_map/all_to_all | solution.py:198
  253.2 3.4 copy-start.5
  254.8 98.5 %collective-permute-start.9 = (f32[2,256,1,128]{3,1,2,0:T(8,128)S(1)}, f32[2,256,1,128]{3,1,2,0:T(8,128)S(1)}, u32[]{:S(2)}, u32[]{:S(2)}) collective-permute-start(f32[2,256,1,128]{3,1,2,0:T(8,128)S(1)} %pad_maximum_fusion.5), channel_id=1, source_target_pairs={{16,0},{17,1},{18,2},{19,3},{20,4},{21,5},{22,6},{23,7},{24,8},{25... | collective-permute-start | bytes 786440 | tf_op jit(solution)/shard_map/ppermute | solution.py:47
  257.4 1.1 copy-start.13
  257.4 1.7 copy-start.7
  259.7 94.9 %copy-start.11 = (bf16[1,24,128,1,128]{4,2,0,1,3:T(8,128)(2,1)S(1)}, bf16[1,24,128,1,128]{4,2,0,1,3:T(8,128)(2,1)}, u32[]{:S(2)}) copy-start(bf16[1,24,128,1,128]{4,2,0,1,3:T(8,128)(2,1)} %copy-done.10) | copy-start | bytes 2359300
  259.9 95.2 %copy-start.14 = (f32[2,10,128,1,128]{4,2,0,3,1:T(8,128)}, f32[2,10,128,1,128]{4,2,0,3,1:T(8,128)S(1)}, u32[]{:S(2)}) copy-start(f32[2,10,128,1,128]{4,2,0,3,1:T(8,128)S(1)} %bitcast_add_fusion) | copy-start | bytes 3932164
  353.3 13.4 %collective-permute-start.10 = (f32[2,256,1,128]{3,1,2,0:T(8,128)S(1)}, f32[2,256,1,128]{3,1,2,0:T(8,128)S(1)}, u32[]{:S(2)}, u32[]{:S(2)}) collective-permute-start(f32[2,256,1,128]{3,1,2,0:T(8,128)S(1)} %fusion.39), channel_id=1, source_target_pairs={{8,0},{9,1},{10,2},{11,3},{12,4},{13,5},{14,6},{15,7},{40,32},{41,... | collective-permute-start | bytes 786440 | tf_op jit(solution)/shard_map/ppermute | solution.py:47
  355.1 31.6 %collective-permute-start.7 = (bf16[2,128,1,128]{3,1,0,2:T(8,128)(2,1)S(1)}, bf16[2,128,1,128]{3,1,0,2:T(8,128)(2,1)S(1)}, u32[]{:S(2)}, u32[]{:S(2)}) collective-permute-start(bf16[2,128,1,128]{3,1,0,2:T(8,128)(2,1)S(1)} %get-tuple-element.49), channel_id=1, source_target_pairs={{0,1},{1,2},{2,3},{3,4},{4,5},{5,6},{6,7},{7,8},{8,9},{9,10},{10,1... | collective-permute-start | bytes 196616 | tf_op jit(solution)/shard_map/ppermute | solution.py:19
  358.6 28.1 %collective-permute-start.8 = (bf16[2,128,1,128]{3,1,0,2:T(8,128)(2,1)S(1)}, bf16[2,128,1,128]{3,1,0,2:T(8,128)(2,1)S(1)}, u32[]{:S(2)}, u32[]{:S(2)}) collective-permute-start(bf16[2,128,1,128]{3,1,0,2:T(8,128)(2,1)S(1)} %get-tuple-element.50), channel_id=1, source_target_pairs={{1,0},{2,1},{3,2},{4,3},{5,4},{6,5},{7,6},{8,7},{9,8},{10,9},{11,1... | collective-permute-start | bytes 196616 | tf_op jit(solution)/shard_map/ppermute | solution.py:21
  366.8 7.9 %collective-permute-start.11 = (f32[2,256,1,128]{3,1,2,0:T(8,128)S(1)}, f32[2,256,1,128]{3,1,2,0:T(8,128)S(1)}, u32[]{:S(2)}, u32[]{:S(2)}) collective-permute-start(f32[2,256,1,128]{3,1,2,0:T(8,128)S(1)} %fusion.61), channel_id=1, source_target_pairs={{4,0},{5,1},{6,2},{7,3},{36,32},{37,33},{38,34},{39,35},{68,64},{6... | collective-permute-start | bytes 786440 | tf_op jit(solution)/shard_map/ppermute | solution.py:47
  369.1 17.6 %copy-start.15 = (f32[2,10,128,1,128]{4,2,0,3,1:T(8,128)S(1)}, f32[2,10,128,1,128]{4,2,0,3,1:T(8,128)}, u32[]{:S(2)}) copy-start(f32[2,10,128,1,128]{4,2,0,3,1:T(8,128)} %copy-done.14) | copy-start | bytes 3932164
  369.1 17.6 %slice-start = ((f32[2,10,128,1,128]{4,2,0,3,1:T(8,128)}), f32[2,8,128,1,128]{4,2,0,3,1:T(8,128)S(1)}, s32[]{:S(2)}) async-start(f32[2,10,128,1,128]{4,2,0,3,1:T(8,128)} %copy-done.14), calls=%async_computation.11 | async-start | bytes 2097152 | tf_op jit(solution)/shard_map/slice | solution.py:184
  374.6 8.6 %collective-permute-start.12 = (f32[2,256,1,128]{3,1,2,0:T(8,128)S(1)}, f32[2,256,1,128]{3,1,2,0:T(8,128)S(1)}, u32[]{:S(2)}, u32[]{:S(2)}) collective-permute-start(f32[2,256,1,128]{3,1,2,0:T(8,128)S(1)} %add.165), channel_id=1, source_target_pairs={{2,0},{3,1},{34,32},{35,33},{66,64},{67,65},{98,96},{99,97},{130,1... | collective-permute-start | bytes 786440 | tf_op jit(solution)/shard_map/ppermute | solution.py:47
  383.3 17.7 %collective-permute-start.13 = (f32[2,256,1,128]{3,1,2,0:T(8,128)S(1)}, f32[2,256,1,128]{3,1,2,0:T(8,128)S(1)}, u32[]{:S(2)}, u32[]{:S(2)}) collective-permute-start(f32[2,256,1,128]{3,1,2,0:T(8,128)S(1)} %add.166), channel_id=1, source_target_pairs={{1,0},{33,32},{65,64},{97,96},{129,128},{161,160},{193,192},{225,2... | collective-permute-start | bytes 786440 | tf_op jit(solution)/shard_map/ppermute | solution.py:47
  390.5 22.4 %all-to-all-start.5 = ((bf16[16,64,128]{2,1,0:T(8,128)(2,1)}), bf16[16,64,128]{2,1,0:T(8,128)(2,1)S(1)}, u32[]{:S(2)}, u32[]{:S(2)}) async-start(bf16[16,64,128]{2,1,0:T(8,128)(2,1)} %bitcast.45), calls=%async_computation.5 | async-start | bytes 524288 | tf_op jit(solution)/shard_map/all_to_all | solution.py:220
  412.9 16.5 %all-to-all-start.7 = ((bf16[16,64,128]{2,1,0:T(8,128)(2,1)}), bf16[16,64,128]{2,1,0:T(8,128)(2,1)S(1)}, u32[]{:S(2)}, u32[]{:S(2)}) async-start(bf16[16,64,128]{2,1,0:T(8,128)(2,1)} %bitcast.67), calls=%async_computation.7 | async-start | bytes 524288 | tf_op jit(solution)/shard_map/all_to_all | solution.py:227
  420.5 39.3 %copy-start.1 = (bf16[64,2048]{1,0:T(8,128)(2,1)S(1)}, bf16[64,2048]{1,0:T(8,128)(2,1)}, u32[]{:S(2)}) copy-start(bf16[64,2048]{1,0:T(8,128)(2,1)} %param.11) | copy-start | bytes 786436
  429.4 14.6 %all-to-all-start.10 = ((bf16[16,64,128]{2,1,0:T(8,128)(2,1)}), bf16[16,64,128]{2,1,0:T(8,128)(2,1)S(1)}, u32[]{:S(2)}, u32[]{:S(2)}) async-start(bf16[16,64,128]{2,1,0:T(8,128)(2,1)} %bitcast.126), calls=%async_computation.10 | async-start | bytes 524288 | tf_op jit(solution)/shard_map/all_to_all | solution.py:235
  443.9 15.1 %all-to-all-start.9 = ((bf16[16,64,128]{2,1,0:T(8,128)(2,1)}), bf16[16,64,128]{2,1,0:T(8,128)(2,1)S(1)}, u32[]{:S(2)}, u32[]{:S(2)}) async-start(bf16[16,64,128]{2,1,0:T(8,128)(2,1)} %bitcast.124), calls=%async_computation.9 | async-start | bytes 524288 | tf_op jit(solution)/shard_map/all_to_all | solution.py:234
where the time goes:
time: 461 us; the launch traced here: 460 us
  waiting for transfers between devices  197 us (43%)
  starting transfers between devices  181 us (39%)
  local copies, waits for them, and re-layouts  52.9 us (11%)
  matrix products  15.5 us (3%)
  other arithmetic  11.9 us (3%)
    ppermute x5, waiting for transfers between devices, reduce_to_first(): value = value + lax.ppermute(value, axis, pairs)  111 us
    ppermute x5, starting transfers between devices, broadcast(): got = lax.ppermute(value, axis, pairs)  84 us
    all_to_all x1, starting transfers between devices, shards(): lax.all_to_all(outgoing.reshape(2, groups, capacity, BLK, head_count, HD)...  17.6 us
    all_to_all x1, starting transfers between devices, shards(): lax.all_to_all(request_table(random_blocks, query_count, groups, capacity...  12.9 us
    all_to_all x1, waiting for transfers between devices, shards(): lax.all_to_all(values, 'head', split_axis=1, concat_axis=0, tiled=True)  11.6 us
    all_to_all x1, starting transfers between devices, shards(): lax.all_to_all(attended.reshape(group_tokens, head_count * HD), 'head', s...  10.5 us
    all_to_all x1, waiting for transfers between devices, shards(): lax.all_to_all(grad_k, 'head', split_axis=0, concat_axis=1, tiled=True)  10.2 us
    all_to_all x1, waiting for transfers between devices, shards(): lax.all_to_all(queries, 'head', split_axis=1, concat_axis=0, tiled=True)  9.99 us
  transfers between devices with their start and end apart: 25, of which 19 were waited for; matrix products, arithmetic and copies ran while one was open for 10% of the time, Pallas kernels for 0%

commit v1 on v0

--- a/solution.py
+++ b/solution.py
@@ -122,7 +122,12 @@
     head_q, head_k, head_v, head_g = (
         lax.all_to_all(queries, "head", split_axis=1, concat_axis=0, tiled=True),
         lax.all_to_all(keys, "head", split_axis=1, concat_axis=0, tiled=True),
-        lax.all_to_all(values, "head", split_axis=1, concat_axis=0, tiled=True),
+        jnp.concatenate(
+            lax.all_to_all(
+                jnp.stack(jnp.split(values, lax.axis_size("head"), axis=1)), "head", 0, 0
+            ),
+            axis=0,
+        ),
         lax.all_to_all(grad_out, "head", split_axis=1, concat_axis=0, tiled=True),
     )
     group_tokens = head_q.shape[0]

time: 461 us -> 475 us (1.030)
  local copies, waits for them, and re-layouts: 52.9 us -> 73.3 us
  waiting for transfers between devices: 197 us -> 185 us
  starting transfers between devices: 181 us -> 186 us
    unnamed x42 -> x55, local copies, waits for them, and re-layouts: 4.32 us -> 24.2 us
    all_to_all x1, waiting for transfers between devices: 6.8 us -> 0.01 us  [shards(): lax.all_to_all(request_table(random_blocks, query_count, groups, capacity...]
  transfers between devices with their start and end apart: 25 -> 25, of which waited for: 19 -> 18; matrix products, arithmetic and copies ran while one was open for 10% -> 14% of each run, Pallas kernels for 0% -> 0%
where the time goes in v1:
time: 475 us; the launch traced here: 473 us
  starting transfers between devices  186 us (39%)
  waiting for transfers between devices  185 us (39%)
  local copies, waits for them, and re-layouts  73.3 us (15%)
  matrix products  15.5 us (3%)
  other arithmetic  11.9 us (3%)
    ppermute x5, waiting for transfers between devices, reduce_to_first(): value = value + lax.ppermute(value, axis, pairs)  111 us
    ppermute x5, starting transfers between devices, broadcast(): got = lax.ppermute(value, axis, pairs)  86 us
    unnamed x55, local copies, waits for them, and re-layouts  24.2 us
    all_to_all x1, starting transfers between devices, shards(): lax.all_to_all(outgoing.reshape(2, groups, capacity, BLK, head_count, HD)...  17.3 us
    all_to_all x1, starting transfers between devices, shards(): lax.all_to_all(request_table(random_blocks, query_count, groups, capacity...  12.9 us
    all_to_all x1, waiting for transfers between devices, shards(): lax.all_to_all(jnp.stack(jnp.split(values, lax.axis_size('head'), axis=1)...  11.6 us
    all_to_all x1, starting transfers between devices, shards(): lax.all_to_all(attended.reshape(group_tokens, head_count * HD), 'head', s...  10.7 us
    all_to_all x1, waiting for transfers between devices, shards(): lax.all_to_all(grad_k, 'head', split_axis=0, concat_axis=1, tiled=True)  10.2 us
  transfers between devices with their start and end apart: 25, of which 18 were waited for; matrix products, arithmetic and copies ran while one was open for 14% of the time, Pallas kernels for 0%

profile of v1, /device:TPU:3, one launch (start us, length us, event | category | flops | bytes accessed | tf_op | source)
XLA Modules:
  0.0 472.9 jit_solution(16439823002671946422)
XLA Ops:
  2.7 12.9 %all-to-all-start.3 = ((s32[32,1,2]{2,1,0:T(1,128)}), s32[32,1,2]{2,1,0:T(1,128)S(1)}, u32[]{:S(2)}, u32[]{:S(2)}) async-start(s32[32,1,2]{2,1,0:T(1,128)} %bitcast.35), calls=%async_computation.3 | async-start | bytes 32768 | tf_op jit(solution)/shard_map/all_to_all | solution.py:149
  32.3 8.3 %all-to-all-start.2 = ((bf16[64,16,128]{2,0,1:T(8,128)(2,1)}), bf16[64,16,128]{2,0,1:T(8,128)(2,1)S(1)}, u32[]{:S(2)}, u32[]{:S(2)}) async-start(bf16[64,16,128]{2,0,1:T(8,128)(2,1)} %copy_bitcast_fusion.8), calls=%async_computation.2 | async-start | bytes 524288 | tf_op jit(solution)/shard_map/all_to_all | solution.py:123
  43.3 1.7 copy_bitcast_fusion.9
  45.0 7.3 %all-to-all-done.2 = bf16[64,16,128]{2,0,1:T(8,128)(2,1)S(1)} async-done(((bf16[64,16,128]{2,0,1:T(8,128)(2,1)}), bf16[64,16,128]{2,0,1:T(8,128)(2,1)S(1)}, u32[]{:S(2)}, u32[]{:S(2)}) %all-to-all-start.2) | async-done | bytes 262176 | tf_op jit(solution)/shard_map/all_to_all | solution.py:123
  52.3 3.4 all-to-all-start
  60.6 6.3 %all-to-all-done = bf16[64,16,128]{2,0,1:T(8,128)(2,1)S(1)} async-done(((bf16[64,16,128]{2,0,1:T(8,128)(2,1)}), bf16[64,16,128]{2,0,1:T(8,128)(2,1)S(1)}, u32[]{:S(2)}, u32[]{:S(2)}) %all-to-all-start) | async-done | bytes 262176 | tf_op jit(solution)/shard_map/all_to_all | solution.py:124
  66.9 3.4 all-to-all-start.1
  70.5 11.6 %all-to-all-done.1 = bf16[16,64,128]{2,1,0:T(8,128)(2,1)S(1)} async-done(((bf16[16,64,128]{2,1,0:T(8,128)(2,1)}), bf16[16,64,128]{2,1,0:T(8,128)(2,1)S(1)}, u32[]{:S(2)}, u32[]{:S(2)}) %all-to-all-start.1) | async-done | bytes 262176 | tf_op jit(solution)/shard_map/all_to_all | solution.py:126
  82.0 3.4 all-to-all-start.6
  85.5 3.1 gather_fusion
  88.6 2.7 copy.164
  91.8 2.5 copy.165
  94.3 2.3 all-to-all-done.6
  96.6 9.3 %all-to-all-start.4 = ((bf16[2,32,2,128,1,128]{5,3,2,0,4,1:T(8,128)(2,1)}), bf16[2,32,2,128,1,128]{5,3,2,0,4,1:T(8,128)(2,1)}, u32[]{:S(2)}, u32[]{:S(2)}) async-start(bf16[2,32,2,128,1,128]{5,3,2,0,4,1:T(8,128)(2,1)} %copy.165), calls=%async_computation.4 | async-start | bytes 8388608 | tf_op jit(solution)/shard_map/all_to_all | solution.py:158
  106.2 3.1 collective-permute-start.5
  109.3 2.2 collective-permute-start.6
  112.8 7.4 %collective-permute-done.5 = bf16[2,128,128]{2,1,0:T(8,128)(2,1)S(1)} collective-permute-done((bf16[2,128,128]{2,1,0:T(8,128)(2,1)S(1)}, bf16[2,128,128]{2,1,0:T(8,128)(2,1)S(1)}, u32[]{:S(2)}, u32[]{:S(2)}) %collective-permute-start.5) | collective-permute-done | bytes 65568 | tf_op jit(solution)/shard_map/ppermute | solution.py:19
  120.3 3.2 collective-permute-done
  123.5 80.7 %collective-permute-start.1 = (bf16[2,256,1,128]{3,1,2,0:T(8,128)(2,1)S(1)}, bf16[2,256,1,128]{3,1,2,0:T(8,128)(2,1)S(1)}, u32[]{:S(2)}, u32[]{:S(2)}) collective-permute-start(bf16[2,256,1,128]{3,1,2,0:T(8,128)(2,1)S(1)} %broadcast_select_fusion.1), channel_id=1, source_target_pairs={{0,2},{1,3},{32,34},{33,35},{64,66},{65,67},{96,98},{97,99},{128,1... | collective-permute-start | bytes 393224 | tf_op jit(solution)/shard_map/ppermute | solution.py:34
  204.6 1.6 collective-permute-done.1
  207.6 1.8 collective-permute-done.2
  211.1 1.6 collective-permute-done.3
  214.2 1.5 convolution_bitcast_fusion.1
  218.2 4.8 %copy.166 = bf16[2,32,2,128,1,128]{5,3,2,1,0,4:T(8,128)(2,1)} copy(bf16[2,32,2,128,1,128]{5,3,2,0,4,1:T(8,128)(2,1)} %all-to-all-done.4) | data formatting | bytes 8388608 | tf_op jit(solution)/shard_map/all_to_all | solution.py:158
  223.0 4.1 gather_fusion.1
  227.1 1.6 bitcast_select_fusion
  233.9 1.9 multiply_reduce_fusion
  235.9 2.3 multiply_convert_fusion
  242.1 6.7 %copy.185 = bf16[2,32,2,128,1,128]{5,2,3,0,4,1:T(2,128)(2,1)} copy(bf16[2,32,2,128,1,128]{5,2,1,3,0,4:T(2,128)(2,1)S(1)} %bitcast.335) | data formatting | bytes 8388608 | tf_op jit(solution)/shard_map/reshape | solution.py:204
  248.8 17.3 %all-to-all-start.8 = ((bf16[2,32,2,128,1,128]{5,2,3,0,4,1:T(2,128)(2,1)}), bf16[2,32,2,128,1,128]{5,2,3,0,4,1:T(2,128)(2,1)}, u32[]{:S(2)}, u32[]{:S(2)}) async-start(bf16[2,32,2,128,1,128]{5,2,3,0,4,1:T(2,128)(2,1)} %copy.185), calls=%async_computation.8 | async-start | bytes 8388608 | tf_op jit(solution)/shard_map/all_to_all | solution.py:203
  273.2 93.2 %collective-permute-done.9 = f32[2,256,1,128]{3,1,2,0:T(8,128)S(1)} collective-permute-done((f32[2,256,1,128]{3,1,2,0:T(8,128)S(1)}, f32[2,256,1,128]{3,1,2,0:T(8,128)S(1)}, u32[]{:S(2)}, u32[]{:S(2)}) %collective-permute-start.9) | collective-permute-done | bytes 262176 | tf_op jit(solution)/shard_map/ppermute | solution.py:47
  368.2 3.5 collective-permute-start.7
  371.7 1.9 collective-permute-start.8
  374.1 5.9 %collective-permute-done.10 = f32[2,256,1,128]{3,1,2,0:T(8,128)S(1)} collective-permute-done((f32[2,256,1,128]{3,1,2,0:T(8,128)S(1)}, f32[2,256,1,128]{3,1,2,0:T(8,128)S(1)}, u32[]{:S(2)}, u32[]{:S(2)}) %collective-permute-start.10) | collective-permute-done | bytes 262176 | tf_op jit(solution)/shard_map/ppermute | solution.py:47
  382.4 5.5 %collective-permute-done.11 = f32[2,256,1,128]{3,1,2,0:T(8,128)S(1)} collective-permute-done((f32[2,256,1,128]{3,1,2,0:T(8,128)S(1)}, f32[2,256,1,128]{3,1,2,0:T(8,128)S(1)}, u32[]{:S(2)}, u32[]{:S(2)}) %collective-permute-start.11) | collective-permute-done | bytes 262176 | tf_op jit(solution)/shard_map/ppermute | solution.py:47
  390.3 6.3 %collective-permute-done.12 = f32[2,256,1,128]{3,1,2,0:T(8,128)S(1)} collective-permute-done((f32[2,256,1,128]{3,1,2,0:T(8,128)S(1)}, f32[2,256,1,128]{3,1,2,0:T(8,128)S(1)}, u32[]{:S(2)}, u32[]{:S(2)}) %collective-permute-start.12) | collective-permute-done | bytes 262176 | tf_op jit(solution)/shard_map/ppermute | solution.py:47
  396.6 2.9 collective-permute-start.13
  400.4 3.0 scatter-add.11
  403.4 10.7 %all-to-all-start.5 = ((bf16[16,64,128]{2,1,0:T(8,128)(2,1)}), bf16[16,64,128]{2,1,0:T(8,128)(2,1)S(1)}, u32[]{:S(2)}, u32[]{:S(2)}) async-start(bf16[16,64,128]{2,1,0:T(8,128)(2,1)} %bitcast.60), calls=%async_computation.5 | async-start | bytes 524288 | tf_op jit(solution)/shard_map/all_to_all | solution.py:225
  414.5 9.0 %copy.186 = bf16[2,32,2,128,1,128]{5,2,1,3,0,4:T(2,128)(2,1)} copy(bf16[2,32,2,128,1,128]{5,2,3,0,4,1:T(2,128)(2,1)} %all-to-all-done.8) | data formatting | bytes 8388608 | tf_op jit(solution)/shard_map/all_to_all | solution.py:203
  423.5 2.5 all-to-all-done.5
  426.0 4.8 %all-to-all-start.7 = ((bf16[16,64,128]{2,1,0:T(8,128)(2,1)}), bf16[16,64,128]{2,1,0:T(8,128)(2,1)S(1)}, u32[]{:S(2)}, u32[]{:S(2)}) async-start(bf16[16,64,128]{2,1,0:T(8,128)(2,1)} %bitcast.82), calls=%async_computation.7 | async-start | bytes 524288 | tf_op jit(solution)/shard_map/all_to_all | solution.py:232
  430.7 2.8 fusion.7
  434.4 8.1 %all-to-all-done.7 = bf16[16,64,128]{2,1,0:T(8,128)(2,1)S(1)} async-done(((bf16[16,64,128]{2,1,0:T(8,128)(2,1)}), bf16[16,64,128]{2,1,0:T(8,128)(2,1)S(1)}, u32[]{:S(2)}, u32[]{:S(2)}) %all-to-all-start.7) | async-done | bytes 262176 | tf_op jit(solution)/shard_map/all_to_all | solution.py:232
  442.4 3.4 all-to-all-start.10
  447.4 9.6 %all-to-all-done.10 = bf16[16,64,128]{2,1,0:T(8,128)(2,1)S(1)} async-done(((bf16[16,64,128]{2,1,0:T(8,128)(2,1)}), bf16[16,64,128]{2,1,0:T(8,128)(2,1)S(1)}, u32[]{:S(2)}, u32[]{:S(2)}) %all-to-all-start.10) | async-done | bytes 262176 | tf_op jit(solution)/shard_map/all_to_all | solution.py:240
  457.0 3.4 all-to-all-start.9
  461.9 10.2 %all-to-all-done.9 = bf16[16,64,128]{2,1,0:T(8,128)(2,1)S(1)} async-done(((bf16[16,64,128]{2,1,0:T(8,128)(2,1)}), bf16[16,64,128]{2,1,0:T(8,128)(2,1)S(1)}, u32[]{:S(2)}, u32[]{:S(2)}) %all-to-all-start.9) | async-done | bytes 262176 | tf_op jit(solution)/shard_map/all_to_all | solution.py:239
  (158 shorter events, 64.5 us)
Async XLA Ops:
  0.6 15.0 %copy-start = (bf16[64,2048]{1,0:T(8,128)(2,1)S(1)}, bf16[64,2048]{1,0:T(8,128)(2,1)}, u32[]{:S(2)}) copy-start(bf16[64,2048]{1,0:T(8,128)(2,1)} %param.11) | copy-start | bytes 786436
  0.6 57.8 %copy-start.16 = (bf16[64,2048]{1,0:T(8,128)(2,1)S(1)}, bf16[64,2048]{1,0:T(8,128)(2,1)}, u32[]{:S(2)}) copy-start(bf16[64,2048]{1,0:T(8,128)(2,1)} %param.14) | copy-start | bytes 786436
  2.7 29.6 %all-to-all-start.3 = ((s32[32,1,2]{2,1,0:T(1,128)}), s32[32,1,2]{2,1,0:T(1,128)S(1)}, u32[]{:S(2)}, u32[]{:S(2)}) async-start(s32[32,1,2]{2,1,0:T(1,128)} %bitcast.35), calls=%async_computation.3 | async-start | bytes 32768 | tf_op jit(solution)/shard_map/all_to_all | solution.py:149
  32.3 20.1 %all-to-all-start.2 = ((bf16[64,16,128]{2,0,1:T(8,128)(2,1)}), bf16[64,16,128]{2,0,1:T(8,128)(2,1)S(1)}, u32[]{:S(2)}, u32[]{:S(2)}) async-start(bf16[64,16,128]{2,0,1:T(8,128)(2,1)} %copy_bitcast_fusion.8), calls=%async_computation.2 | async-start | bytes 524288 | tf_op jit(solution)/shard_map/all_to_all | solution.py:123
  52.3 14.6 %all-to-all-start = ((bf16[64,16,128]{2,0,1:T(8,128)(2,1)}), bf16[64,16,128]{2,0,1:T(8,128)(2,1)S(1)}, u32[]{:S(2)}, u32[]{:S(2)}) async-start(bf16[64,16,128]{2,0,1:T(8,128)(2,1)} %copy_bitcast_fusion.9), calls=%async_computation | async-start | bytes 524288 | tf_op jit(solution)/shard_map/all_to_all | solution.py:124
  66.9 15.1 %all-to-all-start.1 = ((bf16[16,64,128]{2,1,0:T(8,128)(2,1)}), bf16[16,64,128]{2,1,0:T(8,128)(2,1)S(1)}, u32[]{:S(2)}, u32[]{:S(2)}) async-start(bf16[16,64,128]{2,1,0:T(8,128)(2,1)} %constant_dynamic-update-slice_fusion), calls=%async_computation.1 | async-start | bytes 524288 | tf_op jit(solution)/shard_map/all_to_all | solution.py:126
  82.0 14.5 %all-to-all-start.6 = ((bf16[64,16,128]{2,0,1:T(8,128)(2,1)}), bf16[64,16,128]{2,0,1:T(8,128)(2,1)S(1)}, u32[]{:S(2)}, u32[]{:S(2)}) async-start(bf16[64,16,128]{2,0,1:T(8,128)(2,1)} %copy_bitcast_fusion.7), calls=%async_computation.6 | async-start | bytes 524288 | tf_op jit(solution)/shard_map/all_to_all | solution.py:131
  96.6 121.6 %all-to-all-start.4 = ((bf16[2,32,2,128,1,128]{5,3,2,0,4,1:T(8,128)(2,1)}), bf16[2,32,2,128,1,128]{5,3,2,0,4,1:T(8,128)(2,1)}, u32[]{:S(2)}, u32[]{:S(2)}) async-start(bf16[2,32,2,128,1,128]{5,3,2,0,4,1:T(8,128)(2,1)} %copy.165), calls=%async_computation.4 | async-start | bytes 8388608 | tf_op jit(solution)/shard_map/all_to_all | solution.py:158
  106.2 14.0 %collective-permute-start.5 = (bf16[2,128,128]{2,1,0:T(8,128)(2,1)S(1)}, bf16[2,128,128]{2,1,0:T(8,128)(2,1)S(1)}, u32[]{:S(2)}, u32[]{:S(2)}) collective-permute-start(bf16[2,128,128]{2,1,0:T(8,128)(2,1)S(1)} %get-tuple-element.58), channel_id=1, source_target_pairs={{0,1},{1,2},{2,3},{3,4},{4,5},{5,6},{6,7},{7,8},{8,9},{9,10},{10,1... | collective-permute-start | bytes 196616 | tf_op jit(solution)/shard_map/ppermute | solution.py:19
  109.3 10.9 %collective-permute-start.6 = (bf16[2,128,128]{2,1,0:T(8,128)(2,1)S(1)}, bf16[2,128,128]{2,1,0:T(8,128)(2,1)S(1)}, u32[]{:S(2)}, u32[]{:S(2)}) collective-permute-start(bf16[2,128,128]{2,1,0:T(8,128)(2,1)S(1)} %get-tuple-element.59), channel_id=1, source_target_pairs={{1,0},{2,1},{3,2},{4,3},{5,4},{6,5},{7,6},{8,7},{9,8},{10,9},{11,1... | collective-permute-start | bytes 196616 | tf_op jit(solution)/shard_map/ppermute | solution.py:21
  111.5 12.0 %collective-permute-start = (bf16[2,256,1,128]{3,1,2,0:T(8,128)(2,1)S(1)}, bf16[2,256,1,128]{3,1,2,0:T(8,128)(2,1)S(1)}, u32[]{:S(2)}, u32[]{:S(2)}) collective-permute-start(bf16[2,256,1,128]{3,1,2,0:T(8,128)(2,1)S(1)} %bitcast.371), channel_id=1, source_target_pairs={{0,1},{32,33},{64,65},{96,97},{128,129},{160,161},{192,193},{224,2... | collective-permute-start | bytes 393224 | tf_op jit(solution)/shard_map/ppermute | solution.py:34
  123.5 82.6 %collective-permute-start.1 = (bf16[2,256,1,128]{3,1,2,0:T(8,128)(2,1)S(1)}, bf16[2,256,1,128]{3,1,2,0:T(8,128)(2,1)S(1)}, u32[]{:S(2)}, u32[]{:S(2)}) collective-permute-start(bf16[2,256,1,128]{3,1,2,0:T(8,128)(2,1)S(1)} %broadcast_select_fusion.1), channel_id=1, source_target_pairs={{0,2},{1,3},{32,34},{33,35},{64,66},{65,67},{96,98},{97,99},{128,1... | collective-permute-start | bytes 393224 | tf_op jit(solution)/shard_map/ppermute | solution.py:34
  206.1 3.2 collective-permute-start.2
  207.6 8.1 %copy-start.6 = (bf16[2,8,384,1,128]{4,2,1,3,0:T(8,128)(2,1)}, bf16[2,8,384,1,128]{4,2,1,3,0:T(8,128)(2,1)S(1)}, u32[]{:S(2)}) copy-start(bf16[2,8,384,1,128]{4,2,1,3,0:T(8,128)(2,1)S(1)} %pad_maximum_fusion.1) | copy-start | bytes 4718596
  209.4 3.3 collective-permute-start.3
  212.7 3.8 collective-permute-start.4
  228.9 1.8 copy-start.10
  228.9 3.3 copy-start.12
  232.2 1.4 copy-start.8
  232.3 1.7 copy-start.9
  238.2 1.4 copy-start.2
  238.2 2.0 copy-start.4
  248.8 17.4 %copy-start.3 = (bf16[8,1,128,1024]{2,3,0,1:T(8,128)(2,1)S(1)}, bf16[8,1,128,1024]{2,3,0,1:T(8,128)(2,1)}, u32[]{:S(2)}) copy-start(bf16[8,1,128,1024]{2,3,0,1:T(8,128)(2,1)} %copy-done.2) | copy-start | bytes 6291460
  248.8 154.6 %all-to-all-start.8 = ((bf16[2,32,2,128,1,128]{5,2,3,0,4,1:T(2,128)(2,1)}), bf16[2,32,2,128,1,128]{5,2,3,0,4,1:T(2,128)(2,1)}, u32[]{:S(2)}, u32[]{:S(2)}) async-start(bf16[2,32,2,128,1,128]{5,2,3,0,4,1:T(2,128)(2,1)} %copy.185), calls=%async_computation.8 | async-start | bytes 8388608 | tf_op jit(solution)/shard_map/all_to_all | solution.py:203
  266.5 3.4 copy-start.5
  268.0 98.4 %collective-permute-start.9 = (f32[2,256,1,128]{3,1,2,0:T(8,128)S(1)}, f32[2,256,1,128]{3,1,2,0:T(8,128)S(1)}, u32[]{:S(2)}, u32[]{:S(2)}) collective-permute-start(f32[2,256,1,128]{3,1,2,0:T(8,128)S(1)} %pad_maximum_fusion.5), channel_id=1, source_target_pairs={{16,0},{17,1},{18,2},{19,3},{20,4},{21,5},{22,6},{23,7},{24,8},{25... | collective-permute-start | bytes 786440 | tf_op jit(solution)/shard_map/ppermute | solution.py:47
  270.6 1.1 copy-start.13
  270.6 1.7 copy-start.7
  272.9 94.8 %copy-start.11 = (bf16[1,24,128,1,128]{4,2,0,1,3:T(8,128)(2,1)S(1)}, bf16[1,24,128,1,128]{4,2,0,1,3:T(8,128)(2,1)}, u32[]{:S(2)}) copy-start(bf16[1,24,128,1,128]{4,2,0,1,3:T(8,128)(2,1)} %copy-done.10) | copy-start | bytes 2359300
  273.2 95.0 %copy-start.14 = (f32[2,10,128,1,128]{4,2,0,3,1:T(8,128)}, f32[2,10,128,1,128]{4,2,0,3,1:T(8,128)S(1)}, u32[]{:S(2)}) copy-start(f32[2,10,128,1,128]{4,2,0,3,1:T(8,128)S(1)} %bitcast_add_fusion) | copy-start | bytes 3932164
  366.4 13.5 %collective-permute-start.10 = (f32[2,256,1,128]{3,1,2,0:T(8,128)S(1)}, f32[2,256,1,128]{3,1,2,0:T(8,128)S(1)}, u32[]{:S(2)}, u32[]{:S(2)}) collective-permute-start(f32[2,256,1,128]{3,1,2,0:T(8,128)S(1)} %fusion.39), channel_id=1, source_target_pairs={{8,0},{9,1},{10,2},{11,3},{12,4},{13,5},{14,6},{15,7},{40,32},{41,... | collective-permute-start | bytes 786440 | tf_op jit(solution)/shard_map/ppermute | solution.py:47
  368.2 31.3 %collective-permute-start.7 = (bf16[2,128,1,128]{3,1,0,2:T(8,128)(2,1)S(1)}, bf16[2,128,1,128]{3,1,0,2:T(8,128)(2,1)S(1)}, u32[]{:S(2)}, u32[]{:S(2)}) collective-permute-start(bf16[2,128,1,128]{3,1,0,2:T(8,128)(2,1)S(1)} %get-tuple-element.49), channel_id=1, source_target_pairs={{0,1},{1,2},{2,3},{3,4},{4,5},{5,6},{6,7},{7,8},{8,9},{9,10},{10,1... | collective-permute-start | bytes 196616 | tf_op jit(solution)/shard_map/ppermute | solution.py:19
  371.7 27.8 %collective-permute-start.8 = (bf16[2,128,1,128]{3,1,0,2:T(8,128)(2,1)S(1)}, bf16[2,128,1,128]{3,1,0,2:T(8,128)(2,1)S(1)}, u32[]{:S(2)}, u32[]{:S(2)}) collective-permute-start(bf16[2,128,1,128]{3,1,0,2:T(8,128)(2,1)S(1)} %get-tuple-element.50), channel_id=1, source_target_pairs={{1,0},{2,1},{3,2},{4,3},{5,4},{6,5},{7,6},{8,7},{9,8},{10,9},{11,1... | collective-permute-start | bytes 196616 | tf_op jit(solution)/shard_map/ppermute | solution.py:21
  380.0 7.8 %collective-permute-start.11 = (f32[2,256,1,128]{3,1,2,0:T(8,128)S(1)}, f32[2,256,1,128]{3,1,2,0:T(8,128)S(1)}, u32[]{:S(2)}, u32[]{:S(2)}) collective-permute-start(f32[2,256,1,128]{3,1,2,0:T(8,128)S(1)} %fusion.61), channel_id=1, source_target_pairs={{4,0},{5,1},{6,2},{7,3},{36,32},{37,33},{38,34},{39,35},{68,64},{6... | collective-permute-start | bytes 786440 | tf_op jit(solution)/shard_map/ppermute | solution.py:47
  382.4 17.1 %copy-start.15 = (f32[2,10,128,1,128]{4,2,0,3,1:T(8,128)S(1)}, f32[2,10,128,1,128]{4,2,0,3,1:T(8,128)}, u32[]{:S(2)}) copy-start(f32[2,10,128,1,128]{4,2,0,3,1:T(8,128)} %copy-done.14) | copy-start | bytes 3932164
  382.4 17.2 %slice-start = ((f32[2,10,128,1,128]{4,2,0,3,1:T(8,128)}), f32[2,8,128,1,128]{4,2,0,3,1:T(8,128)S(1)}, s32[]{:S(2)}) async-start(f32[2,10,128,1,128]{4,2,0,3,1:T(8,128)} %copy-done.14), calls=%async_computation.11 | async-start | bytes 2097152 | tf_op jit(solution)/shard_map/slice | solution.py:189
  387.9 8.6 %collective-permute-start.12 = (f32[2,256,1,128]{3,1,2,0:T(8,128)S(1)}, f32[2,256,1,128]{3,1,2,0:T(8,128)S(1)}, u32[]{:S(2)}, u32[]{:S(2)}) collective-permute-start(f32[2,256,1,128]{3,1,2,0:T(8,128)S(1)} %add.165), channel_id=1, source_target_pairs={{2,0},{3,1},{34,32},{35,33},{66,64},{67,65},{98,96},{99,97},{130,1... | collective-permute-start | bytes 786440 | tf_op jit(solution)/shard_map/ppermute | solution.py:47
  396.6 17.6 %collective-permute-start.13 = (f32[2,256,1,128]{3,1,2,0:T(8,128)S(1)}, f32[2,256,1,128]{3,1,2,0:T(8,128)S(1)}, u32[]{:S(2)}, u32[]{:S(2)}) collective-permute-start(f32[2,256,1,128]{3,1,2,0:T(8,128)S(1)} %add.166), channel_id=1, source_target_pairs={{1,0},{33,32},{65,64},{97,96},{129,128},{161,160},{193,192},{225,2... | collective-permute-start | bytes 786440 | tf_op jit(solution)/shard_map/ppermute | solution.py:47
  403.4 22.6 %all-to-all-start.5 = ((bf16[16,64,128]{2,1,0:T(8,128)(2,1)}), bf16[16,64,128]{2,1,0:T(8,128)(2,1)S(1)}, u32[]{:S(2)}, u32[]{:S(2)}) async-start(bf16[16,64,128]{2,1,0:T(8,128)(2,1)} %bitcast.60), calls=%async_computation.5 | async-start | bytes 524288 | tf_op jit(solution)/shard_map/all_to_all | solution.py:225
  426.0 16.5 %all-to-all-start.7 = ((bf16[16,64,128]{2,1,0:T(8,128)(2,1)}), bf16[16,64,128]{2,1,0:T(8,128)(2,1)S(1)}, u32[]{:S(2)}, u32[]{:S(2)}) async-start(bf16[16,64,128]{2,1,0:T(8,128)(2,1)} %bitcast.82), calls=%async_computation.7 | async-start | bytes 524288 | tf_op jit(solution)/shard_map/all_to_all | solution.py:232
  433.6 39.3 %copy-start.1 = (bf16[64,2048]{1,0:T(8,128)(2,1)S(1)}, bf16[64,2048]{1,0:T(8,128)(2,1)}, u32[]{:S(2)}) copy-start(bf16[64,2048]{1,0:T(8,128)(2,1)} %param.11) | copy-start | bytes 786436
  442.4 14.6 %all-to-all-start.10 = ((bf16[16,64,128]{2,1,0:T(8,128)(2,1)}), bf16[16,64,128]{2,1,0:T(8,128)(2,1)S(1)}, u32[]{:S(2)}, u32[]{:S(2)}) async-start(bf16[16,64,128]{2,1,0:T(8,128)(2,1)} %bitcast.141), calls=%async_computation.10 | async-start | bytes 524288 | tf_op jit(solution)/shard_map/all_to_all | solution.py:240
  457.0 15.1 %all-to-all-start.9 = ((bf16[16,64,128]{2,1,0:T(8,128)(2,1)}), bf16[16,64,128]{2,1,0:T(8,128)(2,1)S(1)}, u32[]{:S(2)}, u32[]{:S(2)}) async-start(bf16[16,64,128]{2,1,0:T(8,128)(2,1)} %bitcast.139), calls=%async_computation.9 | async-start | bytes 524288 | tf_op jit(solution)/shard_map/all_to_all | solution.py:239
